TPU v7x, 512 devices: a whole 4x8x8 slice. The times are simulated.
512 devices in a mesh: gx: 32 (over x, z), gy: 16 (over y, core).
Axes of the slice: x: 4, y: 8, z: 8, core: 2. Of those that a mesh axis runs over, the one named last changes fastest.
Arguments:
- start_disp: float32 [6, 3, 128, 128, 128], P(None, None, 'gx', 'gy'), may hold values from -6 to 6
- bone_mask: int32 [128, 128, 128], P('gx', 'gy'), may hold values from 0 to 1, as said below
- density: float32 [128, 128, 128], P('gx', 'gy'), may hold values from 0.3 to 1
- load_nodes: int32 [32, 16, 6, 32], P('gx', 'gy'), may hold values from 0 to 31
- load_forces: float32 [32, 16, 6, 3, 32], P('gx', 'gy'), may hold values from -12 to 12
Outputs:
- displacement: float32 [6, 3, 128, 128, 128], P(None, None, 'gx', 'gy')
- new_density: float32 [128, 128, 128], P('gx', 'gy')
Inputs may be any that keep to these rules, and one draw needn't show every extreme that they name: `bone_mask`: 1 marks a bone voxel.
All inputs are finite; a program needn't handle non-finite values.
Results may differ from a plain program's by a relative error of at most 0.0001.
Values sent between devices are 32-bit elements; how exact they have to be, the bound alone decides.
No kernel may reach another device: no remote copies, remote signals or barrier semaphores. Data moves between devices by JAX's collectives and lax.ppermute only.
A program may use at most 64 MiB of HBM per device.

v0:
```python
import jax
import jax.numpy as jnp
import numpy as np
from jax import lax
from jax.sharding import PartitionSpec as P

spring = 0.1
poisson = 0.3
blur_sigma = 2.0
density_cap = 1.0
mean_eps = 1e-06
highest = lax.Precision.HIGHEST


def from_behind(block, axis, distance):
    devices = range(lax.axis_size(axis))
    route = [(i - distance, i) for i in devices if i - distance in devices]
    return lax.ppermute(block, axis, route)


def with_halo(cells, sides, width):
    for axis, dim in sides:
        count = lax.axis_size(axis)
        ends = count - 1
        head = lax.slice_in_dim(cells, 0, width, axis=dim)
        tail = lax.slice_in_dim(cells, cells.shape[dim] - width, cells.shape[dim], axis=dim)
        cells = jnp.concatenate(
            [
                lax.ppermute(tail, axis, [(i, (i + 1) % count) for i in range(ends)]),
                cells,
                lax.ppermute(head, axis, [((i + 1) % count, i) for i in range(ends)]),
            ],
            axis=dim,
        )
    return cells


def hex_stiffness():
    lame_first = poisson / ((1.0 + poisson) * (1.0 - 2.0 * poisson))
    shear_mod = 1.0 / (2.0 * (1.0 + poisson))
    elastic = np.zeros((6, 6))
    elastic[:3, :3] = lame_first
    for axis_id in range(3):
        elastic[axis_id, axis_id] = lame_first + 2.0 * shear_mod
        elastic[axis_id + 3, axis_id + 3] = shear_mod
    points = [0.5 - 0.5 / np.sqrt(3.0), 0.5 + 0.5 / np.sqrt(3.0)]
    stiffness = np.zeros((24, 24))
    for point_x in points:
        for point_y in points:
            for point_z in points:
                coords = (point_x, point_y, point_z)
                strain = np.zeros((6, 24))
                for corner in range(8):
                    offsets = (corner // 4, corner // 2 % 2, corner % 2)
                    shapes = [
                        coords[axis_id] if offsets[axis_id] == 1 else 1.0 - coords[axis_id]
                        for axis_id in range(3)
                    ]
                    slopes = [1.0 if offsets[axis_id] == 1 else -1.0 for axis_id in range(3)]
                    grad_x = slopes[0] * shapes[1] * shapes[2]
                    grad_y = shapes[0] * slopes[1] * shapes[2]
                    grad_z = shapes[0] * shapes[1] * slopes[2]
                    column = 3 * corner
                    strain[0, column] = grad_x
                    strain[1, column + 1] = grad_y
                    strain[2, column + 2] = grad_z
                    strain[3, column] = grad_y
                    strain[3, column + 1] = grad_x
                    strain[4, column + 1] = grad_z
                    strain[4, column + 2] = grad_y
                    strain[5, column] = grad_z
                    strain[5, column + 2] = grad_x
                stiffness += 0.125 * strain.T @ elastic @ strain
    return stiffness


def blur_weights():
    offsets = np.arange(9) - 4.0
    unscaled = np.exp(-offsets * offsets / (2.0 * blur_sigma * blur_sigma))
    return [float(entry) for entry in unscaled / unscaled.sum()]


def blur_valid(values, axis_id, extent):
    weights = blur_weights()
    summed = weights[0] * lax.slice_in_dim(values, 0, extent, axis=axis_id)
    for tap_index in range(1, 9):
        summed = summed + weights[tap_index] * lax.slice_in_dim(
            values, tap_index, tap_index + extent, axis=axis_id
        )
    return summed


def element_disp(node_field):
    size_x = node_field.shape[1] - 1
    size_y = node_field.shape[2] - 1
    size_z = node_field.shape[3] - 1
    corners = []
    for corner in range(8):
        off_x, off_y, off_z = (corner // 4, corner // 2 % 2, corner % 2)
        corners.append(
            node_field[:, off_x : off_x + size_x, off_y : off_y + size_y, off_z : off_z + size_z]
        )
    return jnp.stack(corners).reshape(24, size_x, size_y, size_z)


def element_forces(node_field, modulus, stiffness):
    local_disp = element_disp(node_field)
    local_force = jnp.einsum("ij,jabc->iabc", stiffness, local_disp, precision=highest) * modulus
    local_force = local_force.reshape((8, 3) + modulus.shape)
    summed = jnp.zeros_like(node_field)
    for corner in range(8):
        off_x, off_y, off_z = (corner // 4, corner // 2 % 2, corner % 2)
        summed = summed + jnp.pad(
            local_force[corner],
            ((0, 0), (off_x, 1 - off_x), (off_y, 1 - off_y), (off_z, 1 - off_z)),
        )
    return summed


def element_energy(node_field, stiffness):
    local_disp = element_disp(node_field)
    local_force = jnp.einsum("ij,jabc->iabc", stiffness, local_disp, precision=highest)
    return jnp.sum(local_disp * local_force, axis=0)


def local_gram(left_field, right_field):
    return jnp.einsum("iabcd,jabcd->ij", left_field, right_field, precision=highest)


def global_gram(left_field, right_field):
    return lax.psum(local_gram(left_field, right_field), ("gx", "gy"))


def mix_cases(field, coeffs):
    return jnp.einsum("kabcd,kj->jabcd", field, coeffs, precision=highest)


def solve_spd(matrix, rhs_matrix):
    factor = jnp.linalg.cholesky(matrix)
    matrix_order = matrix.shape[0]
    forward = []
    for row_index in range(matrix_order):
        partial_sum = rhs_matrix[row_index]
        for col_index in range(row_index):
            partial_sum = partial_sum - factor[row_index, col_index] * forward[col_index]
        forward.append(partial_sum / factor[row_index, row_index])
    backward = [None] * matrix_order
    for row_index in reversed(range(matrix_order)):
        partial_sum = forward[row_index]
        for col_index in range(row_index + 1, matrix_order):
            partial_sum = partial_sum - factor[col_index, row_index] * backward[col_index]
        backward[row_index] = partial_sum / factor[row_index, row_index]
    return jnp.stack(backward)


def pad_upper_z(field):
    return jnp.pad(field, ((0, 0), (0, 0), (0, 0), (0, 0), (0, 1)))


def gather_upper(field):
    from_x = from_behind(field[:, :, :1], "gx", -1)
    widened = jnp.concatenate([field, from_x], axis=2)
    from_y = from_behind(widened[:, :, :, :1], "gy", -1)
    return jnp.concatenate([widened, from_y], axis=3)


def return_lower(forces):
    size_x = forces.shape[2] - 1
    size_y = forces.shape[3] - 1
    to_y = from_behind(forces[:, :, :, size_y:], "gy", 1)
    kept = forces[:, :, :, :size_y]
    kept = jnp.concatenate([kept[:, :, :, :1] + to_y, kept[:, :, :, 1:]], axis=3)
    to_x = from_behind(kept[:, :, size_x:], "gx", 1)
    kept = kept[:, :, :size_x]
    return jnp.concatenate([kept[:, :, :1] + to_x, kept[:, :, 1:]], axis=2)


def on_device(start_disp, bone_mask, density, load_nodes, load_forces):
    stiffness = jnp.asarray(hex_stiffness(), jnp.float32)
    modulus = bone_mask.astype(jnp.float32) * density * density
    case_count = start_disp.shape[0]
    size_x = start_disp.shape[2]
    size_y = start_disp.shape[3]
    size_z = start_disp.shape[4]

    def apply_operator(field):
        node_field = pad_upper_z(gather_upper(field))
        forces = lax.map(
            lambda case_field: element_forces(case_field, modulus, stiffness), node_field
        )
        return return_lower(forces[..., :-1]) + spring * field

    slot_ids = jnp.arange(size_x * size_y, dtype=jnp.int32)
    matches = (load_nodes[0, 0][:, :, None] == slot_ids).astype(jnp.float32)
    top_plane = jnp.einsum("cls,ckl->cks", matches, load_forces[0, 0], precision=highest).reshape(
        case_count, 3, size_x, size_y
    )
    applied = apply_operator(start_disp)
    residual = jnp.concatenate(
        [-applied[..., :-1], (top_plane - applied[..., -1])[..., None]], axis=4
    )
    solution = start_disp
    norm_now = global_gram(residual, residual)
    applied = apply_operator(residual)
    step_alpha = solve_spd(global_gram(residual, applied), norm_now)
    solution = solution + mix_cases(residual, step_alpha)
    node_field = pad_upper_z(gather_upper(solution))
    energy = jnp.sum(
        lax.map(lambda case_field: element_energy(case_field, stiffness), node_field), axis=0
    )
    stimulus = modulus * energy
    smooth = blur_valid(with_halo(stimulus, (("gx", 0),), 4), 0, size_x)
    smooth = blur_valid(with_halo(smooth, (("gy", 1),), 4), 1, size_y)
    smooth = blur_valid(jnp.pad(smooth, ((0, 0), (0, 0), (4, 4))), 2, size_z)
    summed = lax.psum(jnp.sum(smooth), ("gx", "gy"))
    mean_stim = summed / (size_x * size_y * size_z * lax.axis_size("gx") * lax.axis_size("gy"))
    new_density = jnp.minimum(density * (0.5 + 0.5 * smooth / (mean_stim + mean_eps)), density_cap)
    return (solution, new_density)


def solution(mesh):
    return jax.shard_map(
        on_device,
        mesh=mesh,
        in_specs=(
            P(None, None, "gx", "gy", None),
            P("gx", "gy", None),
            P("gx", "gy", None),
            P("gx", "gy", None, None),
            P("gx", "gy", None, None, None),
        ),
        out_specs=(P(None, None, "gx", "gy", None), P("gx", "gy", None)),
        check_vma=False,
    )
```

profile of v0, /device:TPU:1, one launch (start us, length us, event | category | flops | bytes accessed | tf_op | source)
XLA Modules:
  0.0 417.8 jit_solution(12601050354318549686)
XLA Ops:
  0.6 0.9 slice.505
  1.5 1.3 collective-permute-start
  2.8 1.0 constant_dynamic-update-slice_fusion.1
  3.8 4.3 %collective-permute-done = f32[6,3,1,8,128]{4,3,2,1,0:T(8,128)S(1)} collective-permute-done((f32[6,3,1,8,128]{4,3,2,1,0:T(8,128)S(1)}, f32[6,3,1,8,128]{4,3,2,1,0:T(8,128)S(1)}, u32[]{:S(2)}, u32[]{:S(2)}) %collective-permute-start) | collective-permute-done | bytes 73760 | tf_op jit(solution)/shard_map/ppermute | solution.py:18
  8.1 8.5 %collective-permute-start.1 = (f32[6,3,5,1,128]{4,3,2,1,0:T(1,128)S(1)}, f32[6,3,5,1,128]{4,3,2,1,0:T(1,128)S(1)}, u32[]{:S(2)}, u32[]{:S(2)}) collective-permute-start(f32[6,3,5,1,128]{4,3,2,1,0:T(1,128)S(1)} %slice.696), channel_id=1, source_target_pairs={{1,0},{2,1},{3,2},{4,3},{5,4},{6,5},{7,6},{8,7},{9,8},{10,9},{11,1... | collective-permute-start | bytes 138248 | tf_op jit(solution)/shard_map/ppermute | solution.py:18
  18.0 46.3 %while.37 = (s32[]{:T(128)}, f32[6,3,5,9,129]{4,0,3,2,1:T(8,128)S(1)}, f32[6,3,5,9,129]{4,3,2,1,0:T(8,128)S(1)}, f32[4,8,128]{2,1,0:T(8,128)S(1)}, s32[]{:T(128)}, /*index=5*/f32[24,24,1,1]{1,0,3,2:T(8,128)S(1)}, s32[]{:T(128)}) while((s32[]{:T(128)}, f32[6,3,5,9,129]{4,0,3,2,1:T(8,128)S(1)}, ...), condition=%wide.region_1.2_spmd.clone, body=%wide.region_0.1_spmd.sunk.clone.sunk | while | flops 28531760 | bytes 3258905 | solution.py:188
  19.8 5.9 %dynamic_update_slice.27 = f32[6,3,5,9,129]{4,0,3,2,1:T(8,128)S(1)} dynamic-update-slice(f32[6,3,5,9,129]{4,0,3,2,1:T(8,128)S(1)} %get-tuple-element.402, f32[1,3,5,9,129]{4,0,3,2,1:T(1,128)S(1)} %copy.116, s32[]{:T(128)} %get-tuple-element.401, s32[]{:T(128)} %constant.103.clone.1..sunk, s32[]{:T(128)} %constant.103.clone.1..sunk, s32[]{:T(128)} %constant.103.clone.1..sunk, s32[]{:T(128)} %constant.103.clone.1..sunk) | dynamic-update-slice | bytes 139324 | tf_op jit(solution)/shard_map/while/body/jit(dynamic_update_index_in_dim)/dynamic_update_slice | solution.py:188
  27.5 5.9 %dynamic_update_slice.27 = f32[6,3,5,9,129]{4,0,3,2,1:T(8,128)S(1)} dynamic-update-slice(f32[6,3,5,9,129]{4,0,3,2,1:T(8,128)S(1)} %get-tuple-element.402, f32[1,3,5,9,129]{4,0,3,2,1:T(1,128)S(1)} %copy.116, s32[]{:T(128)} %get-tuple-element.401, s32[]{:T(128)} %constant.103.clone.1..sunk, s32[]{:T(128)} %constant.103.clone.1..sunk, s32[]{:T(128)} %constant.103.clone.1..sunk, s32[]{:T(128)} %constant.103.clone.1..sunk) | dynamic-update-slice | bytes 139324 | tf_op jit(solution)/shard_map/while/body/jit(dynamic_update_index_in_dim)/dynamic_update_slice | solution.py:188
  35.2 5.9 %dynamic_update_slice.27 = f32[6,3,5,9,129]{4,0,3,2,1:T(8,128)S(1)} dynamic-update-slice(f32[6,3,5,9,129]{4,0,3,2,1:T(8,128)S(1)} %get-tuple-element.402, f32[1,3,5,9,129]{4,0,3,2,1:T(1,128)S(1)} %copy.116, s32[]{:T(128)} %get-tuple-element.401, s32[]{:T(128)} %constant.103.clone.1..sunk, s32[]{:T(128)} %constant.103.clone.1..sunk, s32[]{:T(128)} %constant.103.clone.1..sunk, s32[]{:T(128)} %constant.103.clone.1..sunk) | dynamic-update-slice | bytes 139324 | tf_op jit(solution)/shard_map/while/body/jit(dynamic_update_index_in_dim)/dynamic_update_slice | solution.py:188
  42.9 5.9 %dynamic_update_slice.27 = f32[6,3,5,9,129]{4,0,3,2,1:T(8,128)S(1)} dynamic-update-slice(f32[6,3,5,9,129]{4,0,3,2,1:T(8,128)S(1)} %get-tuple-element.402, f32[1,3,5,9,129]{4,0,3,2,1:T(1,128)S(1)} %copy.116, s32[]{:T(128)} %get-tuple-element.401, s32[]{:T(128)} %constant.103.clone.1..sunk, s32[]{:T(128)} %constant.103.clone.1..sunk, s32[]{:T(128)} %constant.103.clone.1..sunk, s32[]{:T(128)} %constant.103.clone.1..sunk) | dynamic-update-slice | bytes 139324 | tf_op jit(solution)/shard_map/while/body/jit(dynamic_update_index_in_dim)/dynamic_update_slice | solution.py:188
  50.6 5.9 %dynamic_update_slice.27 = f32[6,3,5,9,129]{4,0,3,2,1:T(8,128)S(1)} dynamic-update-slice(f32[6,3,5,9,129]{4,0,3,2,1:T(8,128)S(1)} %get-tuple-element.402, f32[1,3,5,9,129]{4,0,3,2,1:T(1,128)S(1)} %copy.116, s32[]{:T(128)} %get-tuple-element.401, s32[]{:T(128)} %constant.103.clone.1..sunk, s32[]{:T(128)} %constant.103.clone.1..sunk, s32[]{:T(128)} %constant.103.clone.1..sunk, s32[]{:T(128)} %constant.103.clone.1..sunk) | dynamic-update-slice | bytes 139324 | tf_op jit(solution)/shard_map/while/body/jit(dynamic_update_index_in_dim)/dynamic_update_slice | solution.py:188
  58.3 5.9 %dynamic_update_slice.27 = f32[6,3,5,9,129]{4,0,3,2,1:T(8,128)S(1)} dynamic-update-slice(f32[6,3,5,9,129]{4,0,3,2,1:T(8,128)S(1)} %get-tuple-element.402, f32[1,3,5,9,129]{4,0,3,2,1:T(1,128)S(1)} %copy.116, s32[]{:T(128)} %get-tuple-element.401, s32[]{:T(128)} %constant.103.clone.1..sunk, s32[]{:T(128)} %constant.103.clone.1..sunk, s32[]{:T(128)} %constant.103.clone.1..sunk, s32[]{:T(128)} %constant.103.clone.1..sunk) | dynamic-update-slice | bytes 139324 | tf_op jit(solution)/shard_map/while/body/jit(dynamic_update_index_in_dim)/dynamic_update_slice | solution.py:188
  64.3 1.9 collective-permute-start.2
  66.3 1.2 collective-permute-done.2
  67.6 1.3 collective-permute-start.3
  69.7 1.3 collective-permute-done.3
  71.6 1.3 collective-permute-start.4
  72.9 4.8 %collective-permute-done.4 = f32[6,3,1,8,128]{4,0,3,2,1:T(8,128)S(1)} collective-permute-done((f32[6,3,1,8,128]{4,0,3,2,1:T(8,128)S(1)}, f32[6,3,1,8,128]{4,0,3,2,1:T(8,128)S(1)}, u32[]{:S(2)}, u32[]{:S(2)}) %collective-permute-start.4) | collective-permute-done | bytes 73760 | tf_op jit(solution)/shard_map/ppermute | solution.py:18
  77.8 3.6 collective-permute-start.5
  81.4 3.6 collective-permute-done.5
  85.3 47.1 %while.38 = (s32[]{:T(128)}, f32[6,3,5,9,129]{4,0,3,2,1:T(8,128)S(1)}, f32[6,3,5,9,129]{4,0,3,2,1:T(8,128)S(1)}, f32[4,8,128]{2,1,0:T(8,128)S(1)}, s32[]{:T(128)}, /*index=5*/f32[24,24,1,1]{1,0,3,2:T(8,128)S(1)}, s32[]{:T(128)}) while((s32[]{:T(128)}, f32[6,3,5,9,129]{4,0,3,2,1:T(8,128)S(1)}, ...), condition=%wide.region_4.5_spmd.clone, body=%wide.region_3.4_spmd.sunk.clone.sunk | while | flops 28531760 | bytes 3398225 | solution.py:188
  87.2 5.9 %dynamic_update_slice.28 = f32[6,3,5,9,129]{4,0,3,2,1:T(8,128)S(1)} dynamic-update-slice(f32[6,3,5,9,129]{4,0,3,2,1:T(8,128)S(1)} %get-tuple-element.423, f32[1,3,5,9,129]{4,0,3,2,1:T(1,128)S(1)} %copy.119, s32[]{:T(128)} %get-tuple-element.422, s32[]{:T(128)} %constant.103.clone.1..sunk.1, s32[]{:T(128)} %constant.103.clone.1..sunk.1, s32[]{:T(128)} %constant.103.clone.1..sunk.1, ...) | dynamic-update-slice | bytes 139324 | tf_op jit(solution)/shard_map/while/body/jit(dynamic_update_index_in_dim)/dynamic_update_slice | solution.py:188
  95.1 5.9 %dynamic_update_slice.28 = f32[6,3,5,9,129]{4,0,3,2,1:T(8,128)S(1)} dynamic-update-slice(f32[6,3,5,9,129]{4,0,3,2,1:T(8,128)S(1)} %get-tuple-element.423, f32[1,3,5,9,129]{4,0,3,2,1:T(1,128)S(1)} %copy.119, s32[]{:T(128)} %get-tuple-element.422, s32[]{:T(128)} %constant.103.clone.1..sunk.1, s32[]{:T(128)} %constant.103.clone.1..sunk.1, s32[]{:T(128)} %constant.103.clone.1..sunk.1, ...) | dynamic-update-slice | bytes 139324 | tf_op jit(solution)/shard_map/while/body/jit(dynamic_update_index_in_dim)/dynamic_update_slice | solution.py:188
  102.9 5.9 %dynamic_update_slice.28 = f32[6,3,5,9,129]{4,0,3,2,1:T(8,128)S(1)} dynamic-update-slice(f32[6,3,5,9,129]{4,0,3,2,1:T(8,128)S(1)} %get-tuple-element.423, f32[1,3,5,9,129]{4,0,3,2,1:T(1,128)S(1)} %copy.119, s32[]{:T(128)} %get-tuple-element.422, s32[]{:T(128)} %constant.103.clone.1..sunk.1, s32[]{:T(128)} %constant.103.clone.1..sunk.1, s32[]{:T(128)} %constant.103.clone.1..sunk.1, ...) | dynamic-update-slice | bytes 139324 | tf_op jit(solution)/shard_map/while/body/jit(dynamic_update_index_in_dim)/dynamic_update_slice | solution.py:188
  110.7 5.9 %dynamic_update_slice.28 = f32[6,3,5,9,129]{4,0,3,2,1:T(8,128)S(1)} dynamic-update-slice(f32[6,3,5,9,129]{4,0,3,2,1:T(8,128)S(1)} %get-tuple-element.423, f32[1,3,5,9,129]{4,0,3,2,1:T(1,128)S(1)} %copy.119, s32[]{:T(128)} %get-tuple-element.422, s32[]{:T(128)} %constant.103.clone.1..sunk.1, s32[]{:T(128)} %constant.103.clone.1..sunk.1, s32[]{:T(128)} %constant.103.clone.1..sunk.1, ...) | dynamic-update-slice | bytes 139324 | tf_op jit(solution)/shard_map/while/body/jit(dynamic_update_index_in_dim)/dynamic_update_slice | solution.py:188
  118.6 5.9 %dynamic_update_slice.28 = f32[6,3,5,9,129]{4,0,3,2,1:T(8,128)S(1)} dynamic-update-slice(f32[6,3,5,9,129]{4,0,3,2,1:T(8,128)S(1)} %get-tuple-element.423, f32[1,3,5,9,129]{4,0,3,2,1:T(1,128)S(1)} %copy.119, s32[]{:T(128)} %get-tuple-element.422, s32[]{:T(128)} %constant.103.clone.1..sunk.1, s32[]{:T(128)} %constant.103.clone.1..sunk.1, s32[]{:T(128)} %constant.103.clone.1..sunk.1, ...) | dynamic-update-slice | bytes 139324 | tf_op jit(solution)/shard_map/while/body/jit(dynamic_update_index_in_dim)/dynamic_update_slice | solution.py:188
  126.4 5.9 %dynamic_update_slice.28 = f32[6,3,5,9,129]{4,0,3,2,1:T(8,128)S(1)} dynamic-update-slice(f32[6,3,5,9,129]{4,0,3,2,1:T(8,128)S(1)} %get-tuple-element.423, f32[1,3,5,9,129]{4,0,3,2,1:T(1,128)S(1)} %copy.119, s32[]{:T(128)} %get-tuple-element.422, s32[]{:T(128)} %constant.103.clone.1..sunk.1, s32[]{:T(128)} %constant.103.clone.1..sunk.1, s32[]{:T(128)} %constant.103.clone.1..sunk.1, ...) | dynamic-update-slice | bytes 139324 | tf_op jit(solution)/shard_map/while/body/jit(dynamic_update_index_in_dim)/dynamic_update_slice | solution.py:188
  132.4 1.9 collective-permute-start.6
  134.4 1.2 collective-permute-done.6
  135.6 4.7 %collective-permute-start.7 = (f32[6,3,1,8,128]{4,0,3,2,1:T(8,128)S(1)}, f32[6,3,1,8,128]{4,0,3,2,1:T(8,128)S(1)}, u32[]{:S(2)}, u32[]{:S(2)}) collective-permute-start(f32[6,3,1,8,128]{4,0,3,2,1:T(8,128)S(1)} %pad_maximum_fusion.1), channel_id=1, source_target_pairs={{0,16},{16,32},{32,48},{48,64},{64,80},{80,96},{96,112},{112,128},... | collective-permute-start | bytes 221192 | tf_op jit(solution)/shard_map/ppermute | solution.py:18
  140.3 1.1 convolution_bitcast_fusion.2
  141.4 1.0 collective-permute-done.7
  142.4 1.1 convolution_bitcast_fusion.1
  143.5 108.2 %all-reduce.20 = (f32[6,6]{1,0:T(8,128)S(1)}, f32[6,6]{0,1:T(8,128)S(1)}) all-reduce(f32[6,6]{1,0:T(8,128)S(1)} %convolution_bitcast_fusion.2, f32[6,6]{0,1:T(8,128)S(1)} %convolution_bitcast_fusion.1), channel_id=1, replica_groups=mesh['gx'=32,'gy'=16] {'gx','gy'}, use_global_device_ids=true, to_apply=%region_2.3 | all-reduce | flops 72 | bytes 576 | tf_op jit(solution)/shard_map/psum | solution.py:131
  256.3 9.5 %subtract_divide_fusion.6 = (f32[1,6]{1,0:T(1,128)S(1)}, f32[1,6]{1,0:T(1,128)S(1)}, f32[1,6]{1,0:T(1,128)S(1)}, f32[1,6]{1,0:T(1,128)S(1)}, f32[1,6]{1,0:T(1,128)S(1)}) fusion(f32[6,6]{1,0:T(8,128)S(1)} %get-tuple-element.239, f32[]{:T(128)} %bitcast.19, f32[]{:T(128)} %bitcast.18, f32[]{:T(128)} %bitcast.17, f32[]{:T(128)} %bitcast.16, f32[]{:T(128)} %bitcast.15, ...), kind=kLoop, calls=%fused_computation.219 | loop fusion | flops 150 | bytes 300 | tf_op jit(solution)/shard_map/div | solution.py:146
  265.8 12.6 %subtract_divide_fusion = (f32[1,6]{1,0:T(1,128)S(1)}, f32[1,6]{1,0:T(1,128)S(1)}, f32[1,6]{1,0:T(1,128)S(1)}, f32[1,6]{1,0:T(1,128)S(1)}, f32[1,6]{1,0:T(1,128)S(1)}, /*index=5*/f32[1,6]{1,0:T(1,128)S(1)}) fusion(f32[1,6]{1,0:T(1,128)S(1)} %get-tuple-element.253, f32[]{:T(128)} %bitcast.21, f32[]{:T(128)} %bitcast.16, f32[]{:T(128)} %bitcast.12, ...), kind=kLoop, calls=%fused_computation.213 | loop fusion | flops 276 | bytes 372 | tf_op jit(solution)/shard_map/div | solution.py:152
  279.3 1.3 collective-permute-start.8
  280.6 4.1 collective-permute-done.8
  284.6 3.7 collective-permute-start.9
  288.4 3.8 collective-permute-done.9
  292.3 8.5 %while.39 = (s32[]{:T(128)}, f32[6,4,8,128]{3,2,1,0:T(8,128)S(1)}, f32[6,3,5,9,129]{4,0,3,2,1:T(8,128)S(1)}, s32[]{:T(128)}, f32[24,24,1,1]{1,0,3,2:T(8,128)S(1)}) while((s32[]{:T(128)}, f32[6,4,8,128]{3,2,1,0:T(8,128)S(1)}, f32[6,3,5,9,129]{4,0,3,2,1:T(8,128)S(1)}, s32[]{:T(128)}, f32[24,24,1,1]{1,0,3,2:T(8,128)S(1)}) %tuple.141), condition=%wide.region_10.11_spmd.clone, body=%wide.region_8.10_spmd.sunk.clone.sunk | while | flops 28504064 | bytes 1509813 | solution.py:209
  300.8 1.3 collective-permute-start.10
  302.1 1.3 collective-permute-start.11
  303.5 3.4 collective-permute-done.11
  306.9 3.0 collective-permute-start.12
  309.9 1.9 collective-permute-start.13
  312.6 2.3 collective-permute-done.13
  315.7 100.9 %psum.23 = f32[]{:T(128)} all-reduce(f32[]{:T(128)} %get-tuple-element.241), channel_id=1, replica_groups=mesh['gx'=32,'gy'=16] {'gx','gy'}, use_global_device_ids=true, to_apply=%region_13.14 | all-reduce | flops 1 | bytes 8 | tf_op jit(solution)/shard_map/psum | solution.py:215
  (295 shorter events, 38.6 us)
Async XLA Ops:
  1.5 6.6 %collective-permute-start = (f32[6,3,1,8,128]{4,3,2,1,0:T(8,128)S(1)}, f32[6,3,1,8,128]{4,3,2,1,0:T(8,128)S(1)}, u32[]{:S(2)}, u32[]{:S(2)}) collective-permute-start(f32[6,3,1,8,128]{4,3,2,1,0:T(8,128)S(1)} %slice.505), channel_id=1, source_target_pairs={{16,0},{32,16},{48,32},{64,48},{80,64},{96,80},{112,96},{128,112},... | collective-permute-start | bytes 221192 | tf_op jit(solution)/shard_map/ppermute | solution.py:18
  8.1 9.3 %collective-permute-start.1 = (f32[6,3,5,1,128]{4,3,2,1,0:T(1,128)S(1)}, f32[6,3,5,1,128]{4,3,2,1,0:T(1,128)S(1)}, u32[]{:S(2)}, u32[]{:S(2)}) collective-permute-start(f32[6,3,5,1,128]{4,3,2,1,0:T(1,128)S(1)} %slice.696), channel_id=1, source_target_pairs={{1,0},{2,1},{3,2},{4,3},{5,4},{6,5},{7,6},{8,7},{9,8},{10,9},{11,1... | collective-permute-start | bytes 138248 | tf_op jit(solution)/shard_map/ppermute | solution.py:18
  17.3 0.7 copy-start.1
  18.0 48.2 %copy-start.3 = (s32[1,1,6,32]{3,1,2,0:T(1,128)S(1)}, s32[1,1,6,32]{3,1,2,0:T(1,128)}, u32[]{:S(2)}) copy-start(s32[1,1,6,32]{3,1,2,0:T(1,128)} %param.15) | copy-start | bytes 2308
  64.3 4.6 %copy-start.4 = (f32[1,1,6,3,32]{4,1,3,2,0:T(1,128)S(1)}, f32[1,1,6,3,32]{4,1,3,2,0:T(1,128)}, u32[]{:S(2)}) copy-start(f32[1,1,6,3,32]{4,1,3,2,0:T(1,128)} %param.16) | copy-start | bytes 6916
  64.3 3.2 collective-permute-start.2
  66.3 4.7 %copy-start = (f32[6,3,4,8,128]{4,3,2,1,0:T(8,128)S(1)}, f32[6,3,4,8,128]{4,3,2,1,0:T(8,128)}, u32[]{:S(2)}) copy-start(f32[6,3,4,8,128]{4,3,2,1,0:T(8,128)} %param.12) | copy-start | bytes 884740
  67.6 3.4 collective-permute-start.3
  71.6 6.1 %collective-permute-start.4 = (f32[6,3,1,8,128]{4,0,3,2,1:T(8,128)S(1)}, f32[6,3,1,8,128]{4,0,3,2,1:T(8,128)S(1)}, u32[]{:S(2)}, u32[]{:S(2)}) collective-permute-start(f32[6,3,1,8,128]{4,0,3,2,1:T(8,128)S(1)} %fusion.43), channel_id=1, source_target_pairs={{16,0},{32,16},{48,32},{64,48},{80,64},{96,80},{112,96},{128,112},... | collective-permute-start | bytes 221192 | tf_op jit(solution)/shard_map/ppermute | solution.py:18
  77.8 7.3 %collective-permute-start.5 = (f32[6,3,5,1,128]{4,0,3,2,1:T(8,128)S(1)}, f32[6,3,5,1,128]{4,0,3,2,1:T(8,128)S(1)}, u32[]{:S(2)}, u32[]{:S(2)}) collective-permute-start(f32[6,3,5,1,128]{4,0,3,2,1:T(8,128)S(1)} %pad_maximum_fusion.4), channel_id=1, source_target_pairs={{1,0},{2,1},{3,2},{4,3},{5,4},{6,5},{7,6},{8,7},{9,8},{10,9},{11,1... | collective-permute-start | bytes 138248 | tf_op jit(solution)/shard_map/ppermute | solution.py:18
  132.4 3.2 collective-permute-start.6
  135.6 6.8 %collective-permute-start.7 = (f32[6,3,1,8,128]{4,0,3,2,1:T(8,128)S(1)}, f32[6,3,1,8,128]{4,0,3,2,1:T(8,128)S(1)}, u32[]{:S(2)}, u32[]{:S(2)}) collective-permute-start(f32[6,3,1,8,128]{4,0,3,2,1:T(8,128)S(1)} %pad_maximum_fusion.1), channel_id=1, source_target_pairs={{0,16},{16,32},{32,48},{48,64},{64,80},{80,96},{96,112},{112,128},... | collective-permute-start | bytes 221192 | tf_op jit(solution)/shard_map/ppermute | solution.py:18
  279.3 5.4 %collective-permute-start.8 = (f32[6,3,1,8,128]{4,0,3,2,1:T(8,128)S(1)}, f32[6,3,1,8,128]{4,0,3,2,1:T(8,128)S(1)}, u32[]{:S(2)}, u32[]{:S(2)}) collective-permute-start(f32[6,3,1,8,128]{4,0,3,2,1:T(8,128)S(1)} %slice.701), channel_id=1, source_target_pairs={{16,0},{32,16},{48,32},{64,48},{80,64},{96,80},{112,96},{128,112},... | collective-permute-start | bytes 221192 | tf_op jit(solution)/shard_map/ppermute | solution.py:18
  284.6 7.5 %collective-permute-start.9 = (f32[6,3,5,1,128]{4,0,3,2,1:T(8,128)S(1)}, f32[6,3,5,1,128]{4,0,3,2,1:T(8,128)S(1)}, u32[]{:S(2)}, u32[]{:S(2)}) collective-permute-start(f32[6,3,5,1,128]{4,0,3,2,1:T(8,128)S(1)} %pad_maximum_fusion.3), channel_id=1, source_target_pairs={{1,0},{2,1},{3,2},{4,3},{5,4},{6,5},{7,6},{8,7},{9,8},{10,9},{11,1... | collective-permute-start | bytes 138248 | tf_op jit(solution)/shard_map/ppermute | solution.py:18
  292.3 124.9 %copy-start.2 = (f32[4,8,128]{2,1,0:T(8,128)S(1)}, f32[4,8,128]{2,1,0:T(8,128)}, u32[]{:S(2)}) copy-start(f32[4,8,128]{2,1,0:T(8,128)} %param.14) | copy-start | bytes 49156
  300.8 2.6 collective-permute-start.10
  302.1 4.7 %collective-permute-start.11 = (f32[4,8,128]{2,1,0:T(8,128)S(1)}, f32[4,8,128]{2,1,0:T(8,128)S(1)}, u32[]{:S(2)}, u32[]{:S(2)}) collective-permute-start(f32[4,8,128]{2,1,0:T(8,128)S(1)} %mul.463), channel_id=1, source_target_pairs={{16,0},{32,16},{48,32},{64,48},{80,64},{96,80},{112,96},{128,112},... | collective-permute-start | bytes 49160 | tf_op jit(solution)/shard_map/ppermute | solution.py:31
  306.9 5.7 %collective-permute-start.12 = (f32[4,4,128]{2,1,0:T(4,128)S(1)}, f32[4,4,128]{2,1,0:T(4,128)S(1)}, u32[]{:S(2)}, u32[]{:S(2)}) collective-permute-start(f32[4,4,128]{2,1,0:T(4,128)S(1)} %get-tuple-element.270), channel_id=1, source_target_pairs={{0,1},{1,2},{2,3},{3,4},{4,5},{5,6},{6,7},{7,8},{8,9},{9,10},{10,1... | collective-permute-start | bytes 24584 | tf_op jit(solution)/shard_map/ppermute | solution.py:29
  309.9 5.0 %collective-permute-start.13 = (f32[4,4,128]{2,1,0:T(4,128)S(1)}, f32[4,4,128]{2,1,0:T(4,128)S(1)}, u32[]{:S(2)}, u32[]{:S(2)}) collective-permute-start(f32[4,4,128]{2,1,0:T(4,128)S(1)} %get-tuple-element.271), channel_id=1, source_target_pairs={{1,0},{2,1},{3,2},{4,3},{5,4},{6,5},{7,6},{8,7},{9,8},{10,9},{11,1... | collective-permute-start | bytes 24584 | tf_op jit(solution)/shard_map/ppermute | solution.py:31
where the time goes:
time: 419 us; the launch traced here: 418 us
  blocking collectives  209 us (50%)
  local copies, waits for them, and re-layouts  88.3 us (21%)
  starting transfers between devices  37.1 us (9%)
  other arithmetic  31.3 us (7%)
  waiting for transfers between devices  31.1 us (7%)
  matrix products  16.5 us (4%)
    psum x1, blocking collectives, global_gram(): return lax.psum(local_gram(left_field, right_field), ('gx', 'gy'))  108 us
    psum x1, blocking collectives, on_device(): summed = lax.psum(jnp.sum(smooth), ('gx', 'gy'))  101 us
    dynamic_update_slice x24, local copies, waits for them, and re-layouts, apply_operator(): lax.map(lambda case_field: element_forces(case_field, modulus, stiffness)...  73.1 us
    ppermute x10, starting transfers between devices, from_behind(): return lax.ppermute(block, axis, route)  29.5 us
    ppermute x10, waiting for transfers between devices, from_behind(): return lax.ppermute(block, axis, route)  25.4 us
    div x1, other arithmetic, solve_spd(): backward[row_index] = partial_sum / factor[row_index, row_index]  12.6 us
    div x1, other arithmetic, solve_spd(): forward.append(partial_sum / factor[row_index, row_index])  9.49 us
  transfers between devices with their start and end apart: 14, of which 12 were waited for; matrix products, arithmetic and copies ran while one was open for 1% of the time, Pallas kernels for 0%

commit v1 on v0

--- a/solution.py
+++ b/solution.py
@@ -103,32 +103,56 @@
     return jnp.stack(corners).reshape(24, size_x, size_y, size_z)
 
 
+def cases_disp(node_field):
+    size_x = node_field.shape[2] - 1
+    size_y = node_field.shape[3] - 1
+    size_z = node_field.shape[4] - 1
+    corners = []
+    for corner in range(8):
+        off_x, off_y, off_z = (corner // 4, corner // 2 % 2, corner % 2)
+        corners.append(
+            node_field[:, :, off_x : off_x + size_x, off_y : off_y + size_y, off_z : off_z + size_z]
+        )
+    return jnp.stack(corners, axis=1).reshape(
+        (node_field.shape[0], 24, size_x, size_y, size_z)
+    )
+
+
 def element_forces(node_field, modulus, stiffness):
-    local_disp = element_disp(node_field)
-    local_force = jnp.einsum("ij,jabc->iabc", stiffness, local_disp, precision=highest) * modulus
-    local_force = local_force.reshape((8, 3) + modulus.shape)
+    local_disp = cases_disp(node_field)
+    local_force = jnp.einsum("ij,cjabd->ciabd", stiffness, local_disp, precision=highest) * modulus
+    local_force = local_force.reshape((node_field.shape[0], 8, 3) + modulus.shape)
     summed = jnp.zeros_like(node_field)
     for corner in range(8):
         off_x, off_y, off_z = (corner // 4, corner // 2 % 2, corner % 2)
         summed = summed + jnp.pad(
-            local_force[corner],
-            ((0, 0), (off_x, 1 - off_x), (off_y, 1 - off_y), (off_z, 1 - off_z)),
+            local_force[:, corner],
+            ((0, 0), (0, 0), (off_x, 1 - off_x), (off_y, 1 - off_y), (off_z, 1 - off_z)),
         )
     return summed
 
 
 def element_energy(node_field, stiffness):
-    local_disp = element_disp(node_field)
-    local_force = jnp.einsum("ij,jabc->iabc", stiffness, local_disp, precision=highest)
-    return jnp.sum(local_disp * local_force, axis=0)
+    local_disp = cases_disp(node_field)
+    local_force = jnp.einsum("ij,cjabd->ciabd", stiffness, local_disp, precision=highest)
+    return jnp.sum(local_disp * local_force, axis=(0, 1))
 
 
 def local_gram(left_field, right_field):
     return jnp.einsum("iabcd,jabcd->ij", left_field, right_field, precision=highest)
 
 
-def global_gram(left_field, right_field):
-    return lax.psum(local_gram(left_field, right_field), ("gx", "gy"))
+def tree_sum(value):
+    for axis in ("gy", "gx"):
+        count = lax.axis_size(axis)
+        if count & (count - 1):
+            value = lax.psum(value, axis)
+            continue
+        step = 1
+        while step < count:
+            value = value + lax.ppermute(value, axis, [(i, i ^ step) for i in range(count)])
+            step *= 2
+    return value
 
 
 def mix_cases(field, coeffs):
@@ -136,6 +160,14 @@
 
 
 def solve_spd(matrix, rhs_matrix):
+    factor = jnp.linalg.cholesky(matrix)
+    forward = lax.linalg.triangular_solve(factor, rhs_matrix, left_side=True, lower=True)
+    return lax.linalg.triangular_solve(
+        factor, forward, left_side=True, lower=True, transpose_a=True
+    )
+
+
+def solve_spd_rows(matrix, rhs_matrix):
     factor = jnp.linalg.cholesky(matrix)
     matrix_order = matrix.shape[0]
     forward = []
@@ -185,34 +217,32 @@
 
     def apply_operator(field):
         node_field = pad_upper_z(gather_upper(field))
-        forces = lax.map(
-            lambda case_field: element_forces(case_field, modulus, stiffness), node_field
-        )
-        return return_lower(forces[..., :-1]) + spring * field
+        forces = element_forces(node_field, modulus, stiffness)
+        return return_lower(forces[..., :-1]) + spring * field, node_field
 
     slot_ids = jnp.arange(size_x * size_y, dtype=jnp.int32)
     matches = (load_nodes[0, 0][:, :, None] == slot_ids).astype(jnp.float32)
     top_plane = jnp.einsum("cls,ckl->cks", matches, load_forces[0, 0], precision=highest).reshape(
         case_count, 3, size_x, size_y
     )
-    applied = apply_operator(start_disp)
+    applied, start_nodes = apply_operator(start_disp)
     residual = jnp.concatenate(
         [-applied[..., :-1], (top_plane - applied[..., -1])[..., None]], axis=4
     )
-    solution = start_disp
-    norm_now = global_gram(residual, residual)
-    applied = apply_operator(residual)
-    step_alpha = solve_spd(global_gram(residual, applied), norm_now)
-    solution = solution + mix_cases(residual, step_alpha)
-    node_field = pad_upper_z(gather_upper(solution))
-    energy = jnp.sum(
-        lax.map(lambda case_field: element_energy(case_field, stiffness), node_field), axis=0
-    )
+    applied, residual_nodes = apply_operator(residual)
+    grams = tree_sum(
+        jnp.stack([local_gram(residual, residual), local_gram(residual, applied)])
+    )
+    norm_now = grams[0]
+    step_alpha = solve_spd(grams[1], norm_now)
+    solution = start_disp + mix_cases(residual, step_alpha)
+    node_field = start_nodes + mix_cases(residual_nodes, step_alpha)
+    energy = element_energy(node_field, stiffness)
     stimulus = modulus * energy
     smooth = blur_valid(with_halo(stimulus, (("gx", 0),), 4), 0, size_x)
     smooth = blur_valid(with_halo(smooth, (("gy", 1),), 4), 1, size_y)
     smooth = blur_valid(jnp.pad(smooth, ((0, 0), (0, 0), (4, 4))), 2, size_z)
-    summed = lax.psum(jnp.sum(smooth), ("gx", "gy"))
+    summed = tree_sum(jnp.sum(smooth))
     mean_stim = summed / (size_x * size_y * size_z * lax.axis_size("gx") * lax.axis_size("gy"))
     new_density = jnp.minimum(density * (0.5 + 0.5 * smooth / (mean_stim + mean_eps)), density_cap)
     return (solution, new_density)

time: 419 us -> 234 us (0.56)
  the two profiles are of different devices: /device:TPU:1 before, /device:TPU:30 now
where the time goes in v1:
time: 234 us; the launch traced here: 233 us
  starting transfers between devices  97.9 us (42%)
  waiting for transfers between devices  92.3 us (39%)
  matrix products  16.3 us (7%)
  local copies, waits for them, and re-layouts  10.7 us (5%)
  between operations  8.13 us (3%)
  other arithmetic  7.58 us (3%)
    ppermute x18, waiting for transfers between devices, tree_sum(): lax.ppermute(value, axis, [(i, i ^ step) for i in range(count)])  65.3 us
    ppermute x18, starting transfers between devices, tree_sum(): lax.ppermute(value, axis, [(i, i ^ step) for i in range(count)])  53.8 us
    ppermute x8, starting transfers between devices, from_behind(): return lax.ppermute(block, axis, route)  32.7 us
    ppermute x8, waiting for transfers between devices, from_behind(): return lax.ppermute(block, axis, route)  20.5 us
    ppermute x2, starting transfers between devices, with_halo(): lax.ppermute(head, axis, [((i + 1) % count, i) for i in range(ends)])  7.31 us
    dot_general x2, matrix products, element_forces(): jnp.einsum('ij,cjabd->ciabd', stiffness, local_disp, precision=highest)  6.99 us
    ppermute x2, waiting for transfers between devices, with_halo(): lax.ppermute(tail, axis, [(i, (i + 1) % count) for i in range(ends)])  5.55 us
    dot_general x1, matrix products, element_energy(): jnp.einsum('ij,cjabd->ciabd', stiffness, local_disp, precision=highest)  5.05 us
  transfers between devices with their start and end apart: 30, of which 27 were waited for; matrix products, arithmetic and copies ran while one was open for 3% of the time, Pallas kernels for 0%

profile of v1, /device:TPU:30, one launch (start us, length us, event | category | flops | bytes accessed | tf_op | source)
XLA Modules:
  0.0 232.8 jit_solution(5127477655613390881)
XLA Ops:
  1.5 11.2 %collective-permute-start = (f32[6,3,1,8,128]{4,0,3,2,1:T(8,128)S(1)}, f32[6,3,1,8,128]{4,0,3,2,1:T(8,128)S(1)}, u32[]{:S(2)}, u32[]{:S(2)}) collective-permute-start(f32[6,3,1,8,128]{4,0,3,2,1:T(8,128)S(1)} %copy.121), channel_id=1, source_target_pairs={{16,0},{32,16},{48,32},{64,48},{80,64},{96,80},{112,96},{128,112},... | collective-permute-start | bytes 221192 | tf_op jit(solution)/shard_map/ppermute | solution.py:18
  15.1 1.9 collective-permute-start.1
  19.7 3.5 %multiply_bitcast_fusion.1 = f32[6,24,4,8,128]{4,1,3,2,0:T(8,128)S(1)} fusion(f32[24,24,1,1,1]{1,0,4,3,2:T(8,128)S(1)} %copy-done.1, f32[6,24,4,8,128]{4,0,3,2,1:T(8,128)S(1)} %bitcast.215, f32[4,8,128]{2,1,0:T(8,128)S(1)} %multiply_multiply_fusion), kind=kOutput, calls=%fused_computation.7 | convolution fusion | flops 170459136 | bytes 4737280 | tf_op jit(solution)/shard_map/ij,cjabd->ciabd/dot_general | solution.py:123
  26.0 4.8 %collective-permute-start.2 = (f32[6,3,5,1,128]{4,0,3,2,1:T(8,128)S(1)}, f32[6,3,5,1,128]{4,0,3,2,1:T(8,128)S(1)}, u32[]{:S(2)}, u32[]{:S(2)}) collective-permute-start(f32[6,3,5,1,128]{4,0,3,2,1:T(8,128)S(1)} %slice.405), channel_id=1, source_target_pairs={{0,1},{1,2},{2,3},{3,4},{4,5},{5,6},{6,7},{7,8},{8,9},{9,10},{10,1... | collective-permute-start | bytes 138248 | tf_op jit(solution)/shard_map/ppermute | solution.py:18
  31.8 1.9 collective-permute-start.3
  34.5 6.9 %collective-permute-done.3 = f32[6,3,1,8,128]{4,0,3,2,1:T(8,128)S(1)} collective-permute-done((f32[6,3,1,8,128]{4,0,3,2,1:T(8,128)S(1)}, f32[6,3,1,8,128]{4,0,3,2,1:T(8,128)S(1)}, u32[]{:S(2)}, u32[]{:S(2)}) %collective-permute-start.3) | collective-permute-done | bytes 73760 | tf_op jit(solution)/shard_map/ppermute | solution.py:18
  42.0 3.7 %collective-permute-start.4 = (f32[6,3,1,8,128]{4,0,3,2,1:T(8,128)S(1)}, f32[6,3,1,8,128]{4,0,3,2,1:T(8,128)S(1)}, u32[]{:S(2)}, u32[]{:S(2)}) collective-permute-start(f32[6,3,1,8,128]{4,0,3,2,1:T(8,128)S(1)} %fusion.65), channel_id=1, source_target_pairs={{16,0},{32,16},{48,32},{64,48},{80,64},{96,80},{112,96},{128,112},... | collective-permute-start | bytes 221192 | tf_op jit(solution)/shard_map/ppermute | solution.py:18
  45.7 2.8 %collective-permute-done.4 = f32[6,3,1,8,128]{4,0,3,2,1:T(8,128)S(1)} collective-permute-done((f32[6,3,1,8,128]{4,0,3,2,1:T(8,128)S(1)}, f32[6,3,1,8,128]{4,0,3,2,1:T(8,128)S(1)}, u32[]{:S(2)}, u32[]{:S(2)}) %collective-permute-start.4) | collective-permute-done | bytes 73760 | tf_op jit(solution)/shard_map/ppermute | solution.py:18
  48.6 2.1 collective-permute-start.5
  53.5 3.5 %multiply_bitcast_fusion = f32[6,24,4,8,128]{4,1,3,2,0:T(8,128)S(1)} fusion(f32[24,24,1,1,1]{1,0,4,3,2:T(8,128)S(1)} %copy-done.1, f32[6,24,4,8,128]{4,0,3,2,1:T(8,128)S(1)} %bitcast.216, f32[4,8,128]{2,1,0:T(8,128)S(1)} %multiply_multiply_fusion), kind=kOutput, calls=%fused_computation.6 | convolution fusion | flops 170459136 | bytes 4737280 | tf_op jit(solution)/shard_map/ij,cjabd->ciabd/dot_general | solution.py:123
  59.7 5.1 %collective-permute-start.6 = (f32[6,3,5,1,128]{4,0,3,2,1:T(8,128)S(1)}, f32[6,3,5,1,128]{4,0,3,2,1:T(8,128)S(1)}, u32[]{:S(2)}, u32[]{:S(2)}) collective-permute-start(f32[6,3,5,1,128]{4,0,3,2,1:T(8,128)S(1)} %slice.422), channel_id=1, source_target_pairs={{0,1},{1,2},{2,3},{3,4},{4,5},{5,6},{6,7},{7,8},{8,9},{9,10},{10,1... | collective-permute-start | bytes 138248 | tf_op jit(solution)/shard_map/ppermute | solution.py:18
  65.8 1.9 collective-permute-start.7
  68.7 6.5 %collective-permute-done.7 = f32[6,3,1,8,128]{4,0,3,2,1:T(8,128)S(1)} collective-permute-done((f32[6,3,1,8,128]{4,0,3,2,1:T(8,128)S(1)}, f32[6,3,1,8,128]{4,0,3,2,1:T(8,128)S(1)}, u32[]{:S(2)}, u32[]{:S(2)}) %collective-permute-start.7) | collective-permute-done | bytes 73760 | tf_op jit(solution)/shard_map/ppermute | solution.py:18
  76.2 1.9 collective-permute-start.8
  79.3 1.9 collective-permute-start.9
  81.2 3.6 %collective-permute-done.9 = f32[2,6,6]{2,1,0:T(8,128)S(1)} collective-permute-done((f32[2,6,6]{2,1,0:T(8,128)S(1)}, f32[2,6,6]{2,1,0:T(8,128)S(1)}, u32[]{:S(2)}, u32[]{:S(2)}) %collective-permute-start.9) | collective-permute-done | bytes 320 | tf_op jit(solution)/shard_map/ppermute | solution.py:153
  86.7 4.5 %collective-permute-done.10 = f32[2,6,6]{2,1,0:T(8,128)S(1)} collective-permute-done((f32[2,6,6]{2,1,0:T(8,128)S(1)}, f32[2,6,6]{2,1,0:T(8,128)S(1)}, u32[]{:S(2)}, u32[]{:S(2)}) %collective-permute-start.10) | collective-permute-done | bytes 320 | tf_op jit(solution)/shard_map/ppermute | solution.py:153
  91.3 3.9 %collective-permute-start.11 = (f32[2,6,6]{2,1,0:T(8,128)S(1)}, f32[2,6,6]{2,1,0:T(8,128)S(1)}, u32[]{:S(2)}, u32[]{:S(2)}) collective-permute-start(f32[2,6,6]{2,1,0:T(8,128)S(1)} %add.271), channel_id=1, source_target_pairs={{0,8},{1,9},{2,10},{3,11},{4,12},{5,13},{6,14},{7,15},{8,0},{9,1},... | collective-permute-start | bytes 872 | tf_op jit(solution)/shard_map/ppermute | solution.py:153
  95.1 5.6 %collective-permute-done.11 = f32[2,6,6]{2,1,0:T(8,128)S(1)} collective-permute-done((f32[2,6,6]{2,1,0:T(8,128)S(1)}, f32[2,6,6]{2,1,0:T(8,128)S(1)}, u32[]{:S(2)}, u32[]{:S(2)}) %collective-permute-start.11) | collective-permute-done | bytes 320 | tf_op jit(solution)/shard_map/ppermute | solution.py:153
  102.6 3.6 %collective-permute-done.12 = f32[2,6,6]{2,1,0:T(8,128)S(1)} collective-permute-done((f32[2,6,6]{2,1,0:T(8,128)S(1)}, f32[2,6,6]{2,1,0:T(8,128)S(1)}, u32[]{:S(2)}, u32[]{:S(2)}) %collective-permute-start.12) | collective-permute-done | bytes 320 | tf_op jit(solution)/shard_map/ppermute | solution.py:153
  108.2 4.5 %collective-permute-done.13 = f32[2,6,6]{2,1,0:T(8,128)S(1)} collective-permute-done((f32[2,6,6]{2,1,0:T(8,128)S(1)}, f32[2,6,6]{2,1,0:T(8,128)S(1)}, u32[]{:S(2)}, u32[]{:S(2)}) %collective-permute-start.13) | collective-permute-done | bytes 320 | tf_op jit(solution)/shard_map/ppermute | solution.py:153
  114.6 7.5 %collective-permute-done.14 = f32[2,6,6]{2,1,0:T(8,128)S(1)} collective-permute-done((f32[2,6,6]{2,1,0:T(8,128)S(1)}, f32[2,6,6]{2,1,0:T(8,128)S(1)}, u32[]{:S(2)}, u32[]{:S(2)}) %collective-permute-start.14) | collective-permute-done | bytes 320 | tf_op jit(solution)/shard_map/ppermute | solution.py:153
  122.1 2.5 %collective-permute-start.15 = (f32[2,6,6]{2,1,0:T(8,128)S(1)}, f32[2,6,6]{2,1,0:T(8,128)S(1)}, u32[]{:S(2)}, u32[]{:S(2)}) collective-permute-start(f32[2,6,6]{2,1,0:T(8,128)S(1)} %add.275), channel_id=1, source_target_pairs={{0,128},{16,144},{32,160},{48,176},{64,192},{80,208},{96,224},{112... | collective-permute-start | bytes 872 | tf_op jit(solution)/shard_map/ppermute | solution.py:153
  124.6 3.1 %collective-permute-done.15 = f32[2,6,6]{2,1,0:T(8,128)S(1)} collective-permute-done((f32[2,6,6]{2,1,0:T(8,128)S(1)}, f32[2,6,6]{2,1,0:T(8,128)S(1)}, u32[]{:S(2)}, u32[]{:S(2)}) %collective-permute-start.15) | collective-permute-done | bytes 320 | tf_op jit(solution)/shard_map/ppermute | solution.py:153
  127.7 3.2 %collective-permute-start.16 = (f32[2,6,6]{2,1,0:T(8,128)S(1)}, f32[2,6,6]{2,1,0:T(8,128)S(1)}, u32[]{:S(2)}, u32[]{:S(2)}) collective-permute-start(f32[2,6,6]{2,1,0:T(8,128)S(1)} %add.276), channel_id=1, source_target_pairs={{0,256},{16,272},{32,288},{48,304},{64,320},{80,336},{96,352},{112... | collective-permute-start | bytes 872 | tf_op jit(solution)/shard_map/ppermute | solution.py:153
  130.9 3.8 %collective-permute-done.16 = f32[2,6,6]{2,1,0:T(8,128)S(1)} collective-permute-done((f32[2,6,6]{2,1,0:T(8,128)S(1)}, f32[2,6,6]{2,1,0:T(8,128)S(1)}, u32[]{:S(2)}, u32[]{:S(2)}) %collective-permute-start.16) | collective-permute-done | bytes 320 | tf_op jit(solution)/shard_map/ppermute | solution.py:153
  139.4 5.0 %fusion = f32[4,8,128]{2,1,0:T(8,128)S(1)} fusion(f32[6,24,4,8,128]{4,0,3,2,1:T(8,128)S(1)} %bitcast.214, f32[24,24,1,1,1]{1,0,4,3,2:T(8,128)S(1)} %copy-done.1), kind=kOutput, calls=%fused_computation.1 | convolution fusion | flops 171044864 | bytes 2377984 | tf_op jit(solution)/shard_map/ij,cjabd->ciabd/dot_general | solution.py:137
  144.5 3.7 %collective-permute-start.18 = (f32[4,8,128]{2,1,0:T(8,128)S(1)}, f32[4,8,128]{2,1,0:T(8,128)S(1)}, u32[]{:S(2)}, u32[]{:S(2)}) collective-permute-start(f32[4,8,128]{2,1,0:T(8,128)S(1)} %mul.135), channel_id=1, source_target_pairs={{16,0},{32,16},{48,32},{64,48},{80,64},{96,80},{112,96},{128,112},... | collective-permute-start | bytes 49160 | tf_op jit(solution)/shard_map/ppermute | solution.py:31
  148.2 2.2 collective-permute-start.17
  150.4 5.5 %collective-permute-done.17 = f32[4,8,128]{2,1,0:T(8,128)S(1)} collective-permute-done((f32[4,8,128]{2,1,0:T(8,128)S(1)}, f32[4,8,128]{2,1,0:T(8,128)S(1)}, u32[]{:S(2)}, u32[]{:S(2)}) %collective-permute-start.17) | collective-permute-done | bytes 16416 | tf_op jit(solution)/shard_map/ppermute | solution.py:29
  155.9 1.9 collective-permute-start.19
  157.9 3.6 %collective-permute-start.20 = (f32[4,4,128]{2,1,0:T(4,128)S(1)}, f32[4,4,128]{2,1,0:T(4,128)S(1)}, u32[]{:S(2)}, u32[]{:S(2)}) collective-permute-start(f32[4,4,128]{2,1,0:T(4,128)S(1)} %get-tuple-element.27), channel_id=1, source_target_pairs={{1,0},{2,1},{3,2},{4,3},{5,4},{6,5},{7,6},{8,7},{9,8},{10,9},{11,1... | collective-permute-start | bytes 24584 | tf_op jit(solution)/shard_map/ppermute | solution.py:31
  164.6 5.5 %collective-permute-start.21 = (f32[]{:T(128)}, f32[]{:T(128)}, u32[]{:S(2)}, u32[]{:S(2)}) collective-permute-start(f32[]{:T(128)} %get-tuple-element.6), channel_id=1, source_target_pairs={{0,1},{1,0},{2,3},{3,2},{4,5},{5,4},{6,7},{7,6},{8,9},{9,8},{10,11... | collective-permute-start | bytes 20 | tf_op jit(solution)/shard_map/ppermute | solution.py:153
  172.4 3.2 %collective-permute-start.22 = (f32[]{:T(128)}, f32[]{:T(128)}, u32[]{:S(2)}, u32[]{:S(2)}) collective-permute-start(f32[]{:T(128)} %add.305), channel_id=1, source_target_pairs={{0,2},{1,3},{2,0},{3,1},{4,6},{5,7},{6,4},{7,5},{8,10},{9,11},{10,... | collective-permute-start | bytes 20 | tf_op jit(solution)/shard_map/ppermute | solution.py:153
  175.6 2.2 collective-permute-done.22
  178.5 3.2 %collective-permute-start.23 = (f32[]{:T(128)}, f32[]{:T(128)}, u32[]{:S(2)}, u32[]{:S(2)}) collective-permute-start(f32[]{:T(128)} %add.306), channel_id=1, source_target_pairs={{0,4},{1,5},{2,6},{3,7},{4,0},{5,1},{6,2},{7,3},{8,12},{9,13},{10,... | collective-permute-start | bytes 20 | tf_op jit(solution)/shard_map/ppermute | solution.py:153
  181.7 3.1 %collective-permute-done.23 = f32[]{:T(128)} collective-permute-done((f32[]{:T(128)}, f32[]{:T(128)}, u32[]{:S(2)}, u32[]{:S(2)}) %collective-permute-start.23) | collective-permute-done | bytes 36 | tf_op jit(solution)/shard_map/ppermute | solution.py:153
  185.5 3.2 %collective-permute-start.24 = (f32[]{:T(128)}, f32[]{:T(128)}, u32[]{:S(2)}, u32[]{:S(2)}) collective-permute-start(f32[]{:T(128)} %add.307), channel_id=1, source_target_pairs={{0,8},{1,9},{2,10},{3,11},{4,12},{5,13},{6,14},{7,15},{8,0},{9,1},... | collective-permute-start | bytes 20 | tf_op jit(solution)/shard_map/ppermute | solution.py:153
  188.7 6.1 %collective-permute-done.24 = f32[]{:T(128)} collective-permute-done((f32[]{:T(128)}, f32[]{:T(128)}, u32[]{:S(2)}, u32[]{:S(2)}) %collective-permute-start.24) | collective-permute-done | bytes 36 | tf_op jit(solution)/shard_map/ppermute | solution.py:153
  195.5 3.2 %collective-permute-start.25 = (f32[]{:T(128)}, f32[]{:T(128)}, u32[]{:S(2)}, u32[]{:S(2)}) collective-permute-start(f32[]{:T(128)} %add.308), channel_id=1, source_target_pairs={{0,16},{16,0},{32,48},{48,32},{64,80},{80,64},{96,112},{112,96},{1... | collective-permute-start | bytes 20 | tf_op jit(solution)/shard_map/ppermute | solution.py:153
  198.7 2.2 collective-permute-done.25
  201.6 3.2 %collective-permute-start.26 = (f32[]{:T(128)}, f32[]{:T(128)}, u32[]{:S(2)}, u32[]{:S(2)}) collective-permute-start(f32[]{:T(128)} %add.309), channel_id=1, source_target_pairs={{0,32},{16,48},{32,0},{48,16},{64,96},{80,112},{96,64},{112,80},{1... | collective-permute-start | bytes 20 | tf_op jit(solution)/shard_map/ppermute | solution.py:153
  204.8 3.1 %collective-permute-done.26 = f32[]{:T(128)} collective-permute-done((f32[]{:T(128)}, f32[]{:T(128)}, u32[]{:S(2)}, u32[]{:S(2)}) %collective-permute-start.26) | collective-permute-done | bytes 36 | tf_op jit(solution)/shard_map/ppermute | solution.py:153
  208.5 3.2 %collective-permute-start.27 = (f32[]{:T(128)}, f32[]{:T(128)}, u32[]{:S(2)}, u32[]{:S(2)}) collective-permute-start(f32[]{:T(128)} %add.310), channel_id=1, source_target_pairs={{0,64},{16,80},{32,96},{48,112},{64,0},{80,16},{96,32},{112,48},{1... | collective-permute-start | bytes 20 | tf_op jit(solution)/shard_map/ppermute | solution.py:153
  211.7 6.1 %collective-permute-done.27 = f32[]{:T(128)} collective-permute-done((f32[]{:T(128)}, f32[]{:T(128)}, u32[]{:S(2)}, u32[]{:S(2)}) %collective-permute-start.27) | collective-permute-done | bytes 36 | tf_op jit(solution)/shard_map/ppermute | solution.py:153
  218.5 3.7 %collective-permute-start.28 = (f32[]{:T(128)}, f32[]{:T(128)}, u32[]{:S(2)}, u32[]{:S(2)}) collective-permute-start(f32[]{:T(128)} %add.311), channel_id=1, source_target_pairs={{0,128},{16,144},{32,160},{48,176},{64,192},{80,208},{96,224},{112... | collective-permute-start | bytes 20 | tf_op jit(solution)/shard_map/ppermute | solution.py:153
  224.6 4.3 %collective-permute-start.29 = (f32[]{:T(128)}, f32[]{:T(128)}, u32[]{:S(2)}, u32[]{:S(2)}) collective-permute-start(f32[]{:T(128)} %add.312), channel_id=1, source_target_pairs={{0,256},{16,272},{32,288},{48,304},{64,320},{80,336},{96,352},{112... | collective-permute-start | bytes 20 | tf_op jit(solution)/shard_map/ppermute | solution.py:153
  228.9 2.6 %collective-permute-done.29 = f32[]{:T(128)} collective-permute-done((f32[]{:T(128)}, f32[]{:T(128)}, u32[]{:S(2)}, u32[]{:S(2)}) %collective-permute-start.29) | collective-permute-done | bytes 36 | tf_op jit(solution)/shard_map/ppermute | solution.py:153
  (113 shorter events, 39.1 us)
Async XLA Ops:
  1.5 13.5 %collective-permute-start = (f32[6,3,1,8,128]{4,0,3,2,1:T(8,128)S(1)}, f32[6,3,1,8,128]{4,0,3,2,1:T(8,128)S(1)}, u32[]{:S(2)}, u32[]{:S(2)}) collective-permute-start(f32[6,3,1,8,128]{4,0,3,2,1:T(8,128)S(1)} %copy.121), channel_id=1, source_target_pairs={{16,0},{32,16},{48,32},{64,48},{80,64},{96,80},{112,96},{128,112},... | collective-permute-start | bytes 221192 | tf_op jit(solution)/shard_map/ppermute | solution.py:18
  15.1 3.8 %collective-permute-start.1 = (f32[6,3,5,1,128]{4,0,3,2,1:T(8,128)S(1)}, f32[6,3,5,1,128]{4,0,3,2,1:T(8,128)S(1)}, u32[]{:S(2)}, u32[]{:S(2)}) collective-permute-start(f32[6,3,5,1,128]{4,0,3,2,1:T(8,128)S(1)} %slice.390), channel_id=1, source_target_pairs={{1,0},{2,1},{3,2},{4,3},{5,4},{6,5},{7,6},{8,7},{9,8},{10,9},{11,1... | collective-permute-start | bytes 138248 | tf_op jit(solution)/shard_map/ppermute | solution.py:18
  18.9 0.8 copy-start.1
  25.1 5.8 %copy-start.3 = (s32[1,1,6,32]{3,1,2,0:T(1,128)S(1)}, s32[1,1,6,32]{3,1,2,0:T(1,128)}, u32[]{:S(2)}) copy-start(s32[1,1,6,32]{3,1,2,0:T(1,128)} %param.9) | copy-start | bytes 2308
  25.1 8.6 %copy-start.4 = (f32[1,1,6,3,32]{4,1,3,2,0:T(1,128)S(1)}, f32[1,1,6,3,32]{4,1,3,2,0:T(1,128)}, u32[]{:S(2)}) copy-start(f32[1,1,6,3,32]{4,1,3,2,0:T(1,128)} %param.10) | copy-start | bytes 6916
  25.1 16.4 %copy-start = (f32[6,3,4,8,128]{4,3,2,1,0:T(8,128)S(1)}, f32[6,3,4,8,128]{4,3,2,1,0:T(8,128)}, u32[]{:S(2)}) copy-start(f32[6,3,4,8,128]{4,3,2,1,0:T(8,128)} %param.6) | copy-start | bytes 884740
  26.0 5.7 %collective-permute-start.2 = (f32[6,3,5,1,128]{4,0,3,2,1:T(8,128)S(1)}, f32[6,3,5,1,128]{4,0,3,2,1:T(8,128)S(1)}, u32[]{:S(2)}, u32[]{:S(2)}) collective-permute-start(f32[6,3,5,1,128]{4,0,3,2,1:T(8,128)S(1)} %slice.405), channel_id=1, source_target_pairs={{0,1},{1,2},{2,3},{3,4},{4,5},{5,6},{6,7},{7,8},{8,9},{9,10},{10,1... | collective-permute-start | bytes 138248 | tf_op jit(solution)/shard_map/ppermute | solution.py:18
  31.8 9.7 %collective-permute-start.3 = (f32[6,3,1,8,128]{4,0,3,2,1:T(8,128)S(1)}, f32[6,3,1,8,128]{4,0,3,2,1:T(8,128)S(1)}, u32[]{:S(2)}, u32[]{:S(2)}) collective-permute-start(f32[6,3,1,8,128]{4,0,3,2,1:T(8,128)S(1)} %pad_maximum_fusion.6), channel_id=1, source_target_pairs={{0,16},{16,32},{32,48},{48,64},{64,80},{80,96},{96,112},{112,128},... | collective-permute-start | bytes 221192 | tf_op jit(solution)/shard_map/ppermute | solution.py:18
  42.0 6.5 %collective-permute-start.4 = (f32[6,3,1,8,128]{4,0,3,2,1:T(8,128)S(1)}, f32[6,3,1,8,128]{4,0,3,2,1:T(8,128)S(1)}, u32[]{:S(2)}, u32[]{:S(2)}) collective-permute-start(f32[6,3,1,8,128]{4,0,3,2,1:T(8,128)S(1)} %fusion.65), channel_id=1, source_target_pairs={{16,0},{32,16},{48,32},{64,48},{80,64},{96,80},{112,96},{128,112},... | collective-permute-start | bytes 221192 | tf_op jit(solution)/shard_map/ppermute | solution.py:18
  48.6 3.8 %collective-permute-start.5 = (f32[6,3,5,1,128]{4,0,3,2,1:T(8,128)S(1)}, f32[6,3,5,1,128]{4,0,3,2,1:T(8,128)S(1)}, u32[]{:S(2)}, u32[]{:S(2)}) collective-permute-start(f32[6,3,5,1,128]{4,0,3,2,1:T(8,128)S(1)} %pad_maximum_fusion.7), channel_id=1, source_target_pairs={{1,0},{2,1},{3,2},{4,3},{5,4},{6,5},{7,6},{8,7},{9,8},{10,9},{11,1... | collective-permute-start | bytes 138248 | tf_op jit(solution)/shard_map/ppermute | solution.py:18
  59.7 6.0 %collective-permute-start.6 = (f32[6,3,5,1,128]{4,0,3,2,1:T(8,128)S(1)}, f32[6,3,5,1,128]{4,0,3,2,1:T(8,128)S(1)}, u32[]{:S(2)}, u32[]{:S(2)}) collective-permute-start(f32[6,3,5,1,128]{4,0,3,2,1:T(8,128)S(1)} %slice.422), channel_id=1, source_target_pairs={{0,1},{1,2},{2,3},{3,4},{4,5},{5,6},{6,7},{7,8},{8,9},{9,10},{10,1... | collective-permute-start | bytes 138248 | tf_op jit(solution)/shard_map/ppermute | solution.py:18
  65.8 9.4 %collective-permute-start.7 = (f32[6,3,1,8,128]{4,0,3,2,1:T(8,128)S(1)}, f32[6,3,1,8,128]{4,0,3,2,1:T(8,128)S(1)}, u32[]{:S(2)}, u32[]{:S(2)}) collective-permute-start(f32[6,3,1,8,128]{4,0,3,2,1:T(8,128)S(1)} %pad_maximum_fusion.5), channel_id=1, source_target_pairs={{0,16},{16,32},{32,48},{48,64},{64,80},{80,96},{96,112},{112,128},... | collective-permute-start | bytes 221192 | tf_op jit(solution)/shard_map/ppermute | solution.py:18
  76.2 3.1 %collective-permute-start.8 = (f32[2,6,6]{2,1,0:T(8,128)S(1)}, f32[2,6,6]{2,1,0:T(8,128)S(1)}, u32[]{:S(2)}, u32[]{:S(2)}) collective-permute-start(f32[2,6,6]{2,1,0:T(8,128)S(1)} %pad_maximum_fusion.12), channel_id=1, source_target_pairs={{0,1},{1,0},{2,3},{3,2},{4,5},{5,4},{6,7},{7,6},{8,9},{9,8},{10,11... | collective-permute-start | bytes 872 | tf_op jit(solution)/shard_map/ppermute | solution.py:153
  79.3 5.5 %collective-permute-start.9 = (f32[2,6,6]{2,1,0:T(8,128)S(1)}, f32[2,6,6]{2,1,0:T(8,128)S(1)}, u32[]{:S(2)}, u32[]{:S(2)}) collective-permute-start(f32[2,6,6]{2,1,0:T(8,128)S(1)} %fusion.134), channel_id=1, source_target_pairs={{0,2},{1,3},{2,0},{3,1},{4,6},{5,7},{6,4},{7,5},{8,10},{9,11},{10,... | collective-permute-start | bytes 872 | tf_op jit(solution)/shard_map/ppermute | solution.py:153
  84.8 6.4 %collective-permute-start.10 = (f32[2,6,6]{2,1,0:T(8,128)S(1)}, f32[2,6,6]{2,1,0:T(8,128)S(1)}, u32[]{:S(2)}, u32[]{:S(2)}) collective-permute-start(f32[2,6,6]{2,1,0:T(8,128)S(1)} %fusion.148), channel_id=1, source_target_pairs={{0,4},{1,5},{2,6},{3,7},{4,0},{5,1},{6,2},{7,3},{8,12},{9,13},{10,... | collective-permute-start | bytes 872 | tf_op jit(solution)/shard_map/ppermute | solution.py:153
  91.3 9.4 %collective-permute-start.11 = (f32[2,6,6]{2,1,0:T(8,128)S(1)}, f32[2,6,6]{2,1,0:T(8,128)S(1)}, u32[]{:S(2)}, u32[]{:S(2)}) collective-permute-start(f32[2,6,6]{2,1,0:T(8,128)S(1)} %add.271), channel_id=1, source_target_pairs={{0,8},{1,9},{2,10},{3,11},{4,12},{5,13},{6,14},{7,15},{8,0},{9,1},... | collective-permute-start | bytes 872 | tf_op jit(solution)/shard_map/ppermute | solution.py:153
  100.7 5.5 %collective-permute-start.12 = (f32[2,6,6]{2,1,0:T(8,128)S(1)}, f32[2,6,6]{2,1,0:T(8,128)S(1)}, u32[]{:S(2)}, u32[]{:S(2)}) collective-permute-start(f32[2,6,6]{2,1,0:T(8,128)S(1)} %add.272), channel_id=1, source_target_pairs={{0,16},{16,0},{32,48},{48,32},{64,80},{80,64},{96,112},{112,96},{1... | collective-permute-start | bytes 872 | tf_op jit(solution)/shard_map/ppermute | solution.py:153
  106.2 6.4 %collective-permute-start.13 = (f32[2,6,6]{2,1,0:T(8,128)S(1)}, f32[2,6,6]{2,1,0:T(8,128)S(1)}, u32[]{:S(2)}, u32[]{:S(2)}) collective-permute-start(f32[2,6,6]{2,1,0:T(8,128)S(1)} %add.273), channel_id=1, source_target_pairs={{0,32},{16,48},{32,0},{48,16},{64,96},{80,112},{96,64},{112,80},{1... | collective-permute-start | bytes 872 | tf_op jit(solution)/shard_map/ppermute | solution.py:153
  112.7 9.4 %collective-permute-start.14 = (f32[2,6,6]{2,1,0:T(8,128)S(1)}, f32[2,6,6]{2,1,0:T(8,128)S(1)}, u32[]{:S(2)}, u32[]{:S(2)}) collective-permute-start(f32[2,6,6]{2,1,0:T(8,128)S(1)} %add.274), channel_id=1, source_target_pairs={{0,64},{16,80},{32,96},{48,112},{64,0},{80,16},{96,32},{112,48},{1... | collective-permute-start | bytes 872 | tf_op jit(solution)/shard_map/ppermute | solution.py:153
  122.1 5.5 %collective-permute-start.15 = (f32[2,6,6]{2,1,0:T(8,128)S(1)}, f32[2,6,6]{2,1,0:T(8,128)S(1)}, u32[]{:S(2)}, u32[]{:S(2)}) collective-permute-start(f32[2,6,6]{2,1,0:T(8,128)S(1)} %add.275), channel_id=1, source_target_pairs={{0,128},{16,144},{32,160},{48,176},{64,192},{80,208},{96,224},{112... | collective-permute-start | bytes 872 | tf_op jit(solution)/shard_map/ppermute | solution.py:153
  127.7 7.0 %collective-permute-start.16 = (f32[2,6,6]{2,1,0:T(8,128)S(1)}, f32[2,6,6]{2,1,0:T(8,128)S(1)}, u32[]{:S(2)}, u32[]{:S(2)}) collective-permute-start(f32[2,6,6]{2,1,0:T(8,128)S(1)} %add.276), channel_id=1, source_target_pairs={{0,256},{16,272},{32,288},{48,304},{64,320},{80,336},{96,352},{112... | collective-permute-start | bytes 872 | tf_op jit(solution)/shard_map/ppermute | solution.py:153
  139.2 93.0 %copy-start.2 = (f32[4,8,128]{2,1,0:T(8,128)S(1)}, f32[4,8,128]{2,1,0:T(8,128)}, u32[]{:S(2)}) copy-start(f32[4,8,128]{2,1,0:T(8,128)} %param.8) | copy-start | bytes 49156
  144.5 5.9 %collective-permute-start.18 = (f32[4,8,128]{2,1,0:T(8,128)S(1)}, f32[4,8,128]{2,1,0:T(8,128)S(1)}, u32[]{:S(2)}, u32[]{:S(2)}) collective-permute-start(f32[4,8,128]{2,1,0:T(8,128)S(1)} %mul.135), channel_id=1, source_target_pairs={{16,0},{32,16},{48,32},{64,48},{80,64},{96,80},{112,96},{128,112},... | collective-permute-start | bytes 49160 | tf_op jit(solution)/shard_map/ppermute | solution.py:31
  148.2 7.7 %collective-permute-start.17 = (f32[4,8,128]{2,1,0:T(8,128)S(1)}, f32[4,8,128]{2,1,0:T(8,128)S(1)}, u32[]{:S(2)}, u32[]{:S(2)}) collective-permute-start(f32[4,8,128]{2,1,0:T(8,128)S(1)} %mul.135), channel_id=1, source_target_pairs={{0,16},{16,32},{32,48},{48,64},{64,80},{80,96},{96,112},{112,128},... | collective-permute-start | bytes 49160 | tf_op jit(solution)/shard_map/ppermute | solution.py:29
  155.9 6.9 %collective-permute-start.19 = (f32[4,4,128]{2,1,0:T(4,128)S(1)}, f32[4,4,128]{2,1,0:T(4,128)S(1)}, u32[]{:S(2)}, u32[]{:S(2)}) collective-permute-start(f32[4,4,128]{2,1,0:T(4,128)S(1)} %get-tuple-element.26), channel_id=1, source_target_pairs={{0,1},{1,2},{2,3},{3,4},{4,5},{5,6},{6,7},{7,8},{8,9},{9,10},{10,1... | collective-permute-start | bytes 24584 | tf_op jit(solution)/shard_map/ppermute | solution.py:29
  157.9 6.0 %collective-permute-start.20 = (f32[4,4,128]{2,1,0:T(4,128)S(1)}, f32[4,4,128]{2,1,0:T(4,128)S(1)}, u32[]{:S(2)}, u32[]{:S(2)}) collective-permute-start(f32[4,4,128]{2,1,0:T(4,128)S(1)} %get-tuple-element.27), channel_id=1, source_target_pairs={{1,0},{2,1},{3,2},{4,3},{5,4},{6,5},{7,6},{8,7},{9,8},{10,9},{11,1... | collective-permute-start | bytes 24584 | tf_op jit(solution)/shard_map/ppermute | solution.py:31
  164.6 6.4 %collective-permute-start.21 = (f32[]{:T(128)}, f32[]{:T(128)}, u32[]{:S(2)}, u32[]{:S(2)}) collective-permute-start(f32[]{:T(128)} %get-tuple-element.6), channel_id=1, source_target_pairs={{0,1},{1,0},{2,3},{3,2},{4,5},{5,4},{6,7},{7,6},{8,9},{9,8},{10,11... | collective-permute-start | bytes 20 | tf_op jit(solution)/shard_map/ppermute | solution.py:153
  172.4 5.4 %collective-permute-start.22 = (f32[]{:T(128)}, f32[]{:T(128)}, u32[]{:S(2)}, u32[]{:S(2)}) collective-permute-start(f32[]{:T(128)} %add.305), channel_id=1, source_target_pairs={{0,2},{1,3},{2,0},{3,1},{4,6},{5,7},{6,4},{7,5},{8,10},{9,11},{10,... | collective-permute-start | bytes 20 | tf_op jit(solution)/shard_map/ppermute | solution.py:153
  178.5 6.3 %collective-permute-start.23 = (f32[]{:T(128)}, f32[]{:T(128)}, u32[]{:S(2)}, u32[]{:S(2)}) collective-permute-start(f32[]{:T(128)} %add.306), channel_id=1, source_target_pairs={{0,4},{1,5},{2,6},{3,7},{4,0},{5,1},{6,2},{7,3},{8,12},{9,13},{10,... | collective-permute-start | bytes 20 | tf_op jit(solution)/shard_map/ppermute | solution.py:153
  185.5 9.3 %collective-permute-start.24 = (f32[]{:T(128)}, f32[]{:T(128)}, u32[]{:S(2)}, u32[]{:S(2)}) collective-permute-start(f32[]{:T(128)} %add.307), channel_id=1, source_target_pairs={{0,8},{1,9},{2,10},{3,11},{4,12},{5,13},{6,14},{7,15},{8,0},{9,1},... | collective-permute-start | bytes 20 | tf_op jit(solution)/shard_map/ppermute | solution.py:153
  195.5 5.4 %collective-permute-start.25 = (f32[]{:T(128)}, f32[]{:T(128)}, u32[]{:S(2)}, u32[]{:S(2)}) collective-permute-start(f32[]{:T(128)} %add.308), channel_id=1, source_target_pairs={{0,16},{16,0},{32,48},{48,32},{64,80},{80,64},{96,112},{112,96},{1... | collective-permute-start | bytes 20 | tf_op jit(solution)/shard_map/ppermute | solution.py:153
  201.6 6.3 %collective-permute-start.26 = (f32[]{:T(128)}, f32[]{:T(128)}, u32[]{:S(2)}, u32[]{:S(2)}) collective-permute-start(f32[]{:T(128)} %add.309), channel_id=1, source_target_pairs={{0,32},{16,48},{32,0},{48,16},{64,96},{80,112},{96,64},{112,80},{1... | collective-permute-start | bytes 20 | tf_op jit(solution)/shard_map/ppermute | solution.py:153
  208.5 9.3 %collective-permute-start.27 = (f32[]{:T(128)}, f32[]{:T(128)}, u32[]{:S(2)}, u32[]{:S(2)}) collective-permute-start(f32[]{:T(128)} %add.310), channel_id=1, source_target_pairs={{0,64},{16,80},{32,96},{48,112},{64,0},{80,16},{96,32},{112,48},{1... | collective-permute-start | bytes 20 | tf_op jit(solution)/shard_map/ppermute | solution.py:153
  218.5 5.4 %collective-permute-start.28 = (f32[]{:T(128)}, f32[]{:T(128)}, u32[]{:S(2)}, u32[]{:S(2)}) collective-permute-start(f32[]{:T(128)} %add.311), channel_id=1, source_target_pairs={{0,128},{16,144},{32,160},{48,176},{64,192},{80,208},{96,224},{112... | collective-permute-start | bytes 20 | tf_op jit(solution)/shard_map/ppermute | solution.py:153
  224.6 6.9 %collective-permute-start.29 = (f32[]{:T(128)}, f32[]{:T(128)}, u32[]{:S(2)}, u32[]{:S(2)}) collective-permute-start(f32[]{:T(128)} %add.312), channel_id=1, source_target_pairs={{0,256},{16,272},{32,288},{48,304},{64,320},{80,336},{96,352},{112... | collective-permute-start | bytes 20 | tf_op jit(solution)/shard_map/ppermute | solution.py:153
